TPU v7x, 128 devices: a whole 4x4x4 slice. The times are simulated.
128 devices in a mesh: dp: 32 (over y, z, core), mp: 4 (over x).
Axes of the slice: x: 4, y: 4, z: 4, core: 2. Of those that a mesh axis runs over, the one named last changes fastest.
Arguments:
- hidden_rows: bfloat16 [16384, 4096], P('dp', 'mp'), may hold values from -3 to 3
- destination: int32 [16384], P('dp'), may hold values from 0 to 16383, as said below
- doc_ids: int32 [16384], P('dp'), may hold values from 0 to 63, never falling along the last dimension, each value on 1 to 8704 neighbouring positions
- norm_gain: float32 [4096], replicated, may hold values from 0.1 to 1.9
- w_query: bfloat16 [4096, 2048], P(None, 'mp'), may hold values from -1 to 1
- w_key: bfloat16 [4096, 512], P(None, 'mp'), may hold values from -1 to 1
- w_value: bfloat16 [4096, 512], P(None, 'mp'), may hold values from -0.09375 to 0.09375
- w_out: bfloat16 [2048, 4096], P('mp'), may hold values from -0.125 to 0.125
Outputs:
- layer_out: bfloat16 [16384, 4096], P('dp', 'mp')
Inputs may be any that keep to these rules, and one draw needn't show every extreme that they name: `destination`: A permutation of the rows. Each aligned block of 512 rows sends exactly 32 rows to each of half of the 512-row blocks of document order and none to the other half, and each block of document order receives exactly 32 rows from each of half of the blocks of token order.
All inputs are finite; a program needn't handle non-finite values.
Results may differ from a plain program's by a relative error of at most 0.011.
Values may be sent and summed in bfloat16 or wider, within the bound.
No kernel may reach another device: no remote copies, remote signals or barrier semaphores. Data moves between devices by JAX's collectives and lax.ppermute only.
A program may use at most 128 MiB of HBM per device.

v0:
```python
import math
import jax
import jax.numpy as jnp
from jax import lax
from jax.sharding import PartitionSpec as P

HD = 128
ROPE_BASE = 500000.0
NORM_EPS = 1e-05
NEG_START = -1e30
key_block = 512


def rope_angles(row_index):
    lane_index = jnp.arange(HD // 2, dtype=jnp.float32)
    frequency = jnp.power(jnp.float32(ROPE_BASE), -2.0 * lane_index / HD)
    return row_index.astype(jnp.float32)[:, None] * frequency[None, :]


def rotate(head_values, angles):
    half_width = head_values.shape[-1] // 2
    first_half = head_values[..., :half_width]
    second_half = head_values[..., half_width:]
    cosine = jnp.cos(angles)[:, None, :]
    sine_part = jnp.sin(angles)[:, None, :]
    return jnp.concatenate(
        [
            first_half * cosine - second_half * sine_part,
            second_half * cosine + first_half * sine_part,
        ],
        axis=-1,
    )


def normalize(routed, norm_gain):
    wide_rows = routed.astype(jnp.float32)
    inv_rms = lax.rsqrt(jnp.mean(wide_rows * wide_rows, axis=1, keepdims=True) + NORM_EPS)
    return (wide_rows * inv_rms * norm_gain[None, :]).astype(jnp.bfloat16)


def local(hidden_rows, destination, doc_ids, norm_gain, w_query, w_key, w_value, w_out):
    owners = lax.axis_size("dp")
    my_index = lax.axis_index("dp")
    tok_dev, columns = hidden_rows.shape
    capacity = 2 * tok_dev // owners
    target = destination // tok_dev
    owner_ids = jnp.arange(owners, dtype=jnp.int32)
    one_hot = (target[:, None] == owner_ids[None, :]).astype(jnp.int32)
    slot_rank = jnp.sum((jnp.cumsum(one_hot, axis=0) - 1) * one_hot, axis=1)
    flat_slot = target * capacity + slot_rank
    outgoing = (
        jnp.zeros((owners * capacity, columns), hidden_rows.dtype).at[flat_slot].set(hidden_rows)
    )
    places = (
        jnp.full((owners * capacity,), tok_dev, jnp.int32).at[flat_slot].set(destination % tok_dev)
    )
    arrived, arrived_rows = (
        lax.all_to_all(
            outgoing.reshape(owners, capacity, columns),
            "dp",
            split_axis=0,
            concat_axis=0,
            tiled=True,
        ),
        lax.all_to_all(
            places.reshape(owners, capacity), "dp", split_axis=0, concat_axis=0, tiled=True
        ),
    )
    arrived_rows = arrived_rows.reshape(-1)
    routed_part = (
        jnp.zeros((tok_dev, columns), hidden_rows.dtype)
        .at[arrived_rows]
        .set(arrived.reshape(-1, columns), mode="drop")
    )
    routed = lax.all_gather(routed_part, "mp", axis=1, tiled=True)
    normed = normalize(routed, norm_gain)
    heads_dev = w_query.shape[1] // HD
    kv_dev = w_key.shape[1] // HD
    group_size = heads_dev // kv_dev
    query_rows = my_index * tok_dev + jnp.arange(tok_dev, dtype=jnp.int32)
    angles = rope_angles(query_rows)
    queries = jnp.dot(normed, w_query, preferred_element_type=jnp.float32).reshape(
        tok_dev, heads_dev, HD
    )
    queries = rotate(queries, angles).astype(jnp.bfloat16).reshape(tok_dev, kv_dev, group_size, HD)
    keys_own = jnp.dot(normed, w_key, preferred_element_type=jnp.float32).reshape(
        tok_dev, kv_dev, HD
    )
    keys_own = rotate(keys_own, angles).astype(jnp.bfloat16)
    values_own = (
        jnp.dot(normed, w_value, preferred_element_type=jnp.float32)
        .astype(jnp.bfloat16)
        .reshape(tok_dev, kv_dev, HD)
    )
    score_scale = HD ** (-0.5)
    query_first = doc_ids[0]
    query_last = doc_ids[tok_dev - 1]
    last_row = query_rows[tok_dev - 1]

    def attend_block(soft_state, block_in):
        keys_blk, values_blk, ids_blk, key_rows = block_in
        row_best, row_total, weighted = soft_state
        scores = (
            jnp.einsum("qgrd,kgd->grqk", queries, keys_blk, preferred_element_type=jnp.float32)
            * score_scale
        )
        allowed = (doc_ids[:, None] == ids_blk[None, :]) & (
            key_rows[None, :] <= query_rows[:, None]
        )
        scores = jnp.where(allowed[None, None], scores, -jnp.inf)
        new_best = jnp.maximum(row_best, jnp.max(scores, axis=-1))
        rescale = jnp.exp(row_best - new_best)
        exp_scores = jnp.exp(scores - new_best[..., None])
        row_total = row_total * rescale + jnp.sum(exp_scores, axis=-1)
        weighted = weighted * rescale[..., None] + jnp.einsum(
            "grqk,kgd->grqd",
            exp_scores.astype(jnp.bfloat16),
            values_blk,
            preferred_element_type=jnp.float32,
        )
        return ((new_best, row_total, weighted), None)

    start_state = (
        jnp.full((kv_dev, group_size, tok_dev), NEG_START, jnp.float32),
        jnp.zeros((kv_dev, group_size, tok_dev), jnp.float32),
        jnp.zeros((kv_dev, group_size, tok_dev, HD), jnp.float32),
    )
    first_row = jnp.int32(0)
    keys_piece = lax.all_gather(keys_own, "dp", axis=0, tiled=True)
    values_piece = lax.all_gather(values_own, "dp", axis=0, tiled=True)
    ids_piece = lax.all_gather(doc_ids, "dp", axis=0, tiled=True)
    key_count = keys_piece.shape[0]
    block_len = math.gcd(key_count, key_block)
    step_count = key_count // block_len
    relevant = (
        (first_row >= 0)
        & (first_row <= last_row)
        & (ids_piece[key_count - 1] >= query_first)
        & (ids_piece[0] <= query_last)
    )

    def run_piece(state_in):
        rows_piece = jnp.arange(key_count, dtype=jnp.int32)
        blocks_in = (
            keys_piece.reshape(step_count, block_len, kv_dev, HD),
            values_piece.reshape(step_count, block_len, kv_dev, HD),
            ids_piece.reshape(step_count, block_len),
            rows_piece.reshape(step_count, block_len),
        )
        return lax.scan(attend_block, state_in, blocks_in)[0]

    def keep_state(state_in):
        return state_in

    soft_state = lax.cond(relevant, run_piece, keep_state, start_state)
    row_best, row_total, weighted = soft_state
    context = (
        jnp.transpose(weighted / row_total[..., None], (2, 0, 1, 3))
        .reshape(tok_dev, heads_dev * HD)
        .astype(jnp.bfloat16)
    )
    partial_out = jnp.dot(context, w_out, preferred_element_type=jnp.float32)
    summed = lax.psum_scatter(partial_out, "mp", scatter_dimension=1, tiled=True)
    attended = (routed_part.astype(jnp.float32) + summed).astype(jnp.bfloat16)
    backward = attended[jnp.minimum(arrived_rows, tok_dev - 1)].reshape(owners, capacity, columns)
    returned = lax.all_to_all(backward, "dp", split_axis=0, concat_axis=0, tiled=True)
    return returned.reshape(owners * capacity, columns)[flat_slot]


def solution(mesh):
    in_specs = (
        P("dp", "mp"),
        P("dp"),
        P("dp"),
        P(),
        P(None, "mp"),
        P(None, "mp"),
        P(None, "mp"),
        P("mp", None),
    )
    out_specs = P("dp", "mp")
    return jax.shard_map(local, mesh=mesh, in_specs=in_specs, out_specs=out_specs, check_vma=False)
```

profile of v0, /device:TPU:1, one launch (start us, length us, event | category | flops | bytes accessed | tf_op | source)
XLA Modules:
  0.0 689.3 jit_solution(14763836879183577752)
XLA Ops:
  12.0 9.6 %all-to-all-start = ((s32[32,1,32]{2,1,0:T(1,128)}), s32[32,1,32]{2,1,0:T(1,128)S(1)}, u32[]{:S(2)}, u32[]{:S(2)}) async-start(s32[32,1,32]{2,1,0:T(1,128)} %all_to_all.12), calls=%async_computation | async-start | bytes 32768 | tf_op jit(solution)/shard_map/all_to_all | solution.py:65
  21.6 4.8 scatter_custom_fusion.1
  28.5 5.3 all-to-all-start.1
  35.2 26.9 %all-to-all-done.1 = bf16[32,32,1024]{2,1,0:T(8,128)(2,1)S(1)} async-done(((bf16[32,32,1024]{2,1,0:T(8,128)(2,1)}), bf16[32,32,1024]{2,1,0:T(8,128)(2,1)S(1)}, u32[]{:S(2)}, u32[]{:S(2)}) %all-to-all-start.1) | async-done | bytes 2097184 | tf_op jit(solution)/shard_map/all_to_all | solution.py:58
  62.1 6.2 scatter_custom_fusion.2
  68.5 45.7 %all-gather.6.cloned.1.call-done = bf16[512,4096]{1,0:T(8,128)(2,1)} async-done(((bf16[512,1024]{1,0:T(8,128)(2,1)}), bf16[512,4096]{1,0:T(8,128)(2,1)}) %all-gather.6.cloned.1.call-update) | async-done | bytes 4194320 | tf_op jit(solution)/shard_map/all_gather | solution.py:75
  120.8 4.2 convolution_convert_fusion
  125.6 24.9 %all-gather.1 = s32[32,1,512]{2,1,0:T(1,128)S(1)} all-gather(s32[1,1,512]{2,1,0:T(1,128)S(1)} %bitcast.137), channel_id=1, replica_groups=mesh['dp'=32,'mp'=4] {'dp'}, dimensions={0}, use_global_device_ids=true | all-gather | bytes 67584 | tf_op jit(solution)/shard_map/all_gather | solution.py:131
  156.4 6.2 fusion.48
  166.8 4.1 all-gather.8.cloned.1.call-done
  170.9 48.1 %all-gather.10.cloned.1.call-done = bf16[16384,128]{1,0:T(8,128)(2,1)} async-done(((bf16[512,128]{1,0:T(8,128)(2,1)}), bf16[16384,128]{1,0:T(8,128)(2,1)}) %all-gather.10.cloned.1.call-update) | async-done | bytes 4194320 | tf_op jit(solution)/shard_map/all_gather | solution.py:130
  219.0 329.5 %conditional.1 = (f32[1,4,512]{2,1,0:T(4,128)}, f32[1,4,512,128]{2,3,1,0:T(8,128)S(1)}) conditional(s32[]{:T(128)} %bitcast.9, () %tuple.17, (bf16[16384,1,128]{0,2,1:T(8,128)(2,1)}, bf16[16384,1,128]{2,0,1:T(8,128)(2,1)}, s32[16384]{0:T(1024)S(1)}, s32[512]{0:T(512)S(1)}, s32[512]{0:T(512)S(1)}, ...), branch_computations={%region_7.8_spmd, %region_8.13_spmd} | conditional | flops 550023168 | bytes 48317764 | solution.py:155
  219.0 6.4 copy.23
  225.4 320.3 %while.14 = (s32[]{:T(128)}, f32[1,4,512]{2,1,0:T(4,128)S(1)}, f32[1,4,512]{2,1,0:T(4,128)}, f32[1,4,512,128]{3,2,1,0:T(8,128)S(1)}, s32[512]{0:T(512)S(1)}, /*i...) while((s32[]{:T(128)}, f32[1,4,512]{2,1,0:T(4,128)S(1)}, ...), condition=%wide.region_12.12_spmd.clone, body=%wide.region_9.11_spmd.clone.sunk | while | flops 549990400 | bytes 33440936 | solution.py:150
  248.8 3.8 fusion.72
  258.8 3.8 fusion.72
  268.8 3.8 fusion.72
  278.9 3.8 fusion.72
  288.9 3.8 fusion.72
  298.9 3.8 fusion.72
  309.0 3.8 fusion.72
  319.0 3.8 fusion.72
  329.0 3.8 fusion.72
  339.0 3.8 fusion.72
  349.1 3.8 fusion.72
  359.1 3.8 fusion.72
  369.1 3.8 fusion.72
  379.2 3.8 fusion.72
  389.2 3.8 fusion.72
  399.2 3.8 fusion.72
  409.3 3.8 fusion.72
  419.3 3.8 fusion.72
  429.3 3.8 fusion.72
  439.3 3.8 fusion.72
  449.4 3.8 fusion.72
  459.4 3.8 fusion.72
  469.4 3.8 fusion.72
  479.5 3.8 fusion.72
  489.5 3.8 fusion.72
  499.5 3.8 fusion.72
  519.6 3.8 fusion.72
  529.6 3.8 fusion.72
  539.6 3.8 fusion.72
  549.4 7.8 %fusion.55 = f32[512,4096]{1,0:T(8,128)} fusion(bf16[512,512]{0,1:T(8,128)(2,1)S(1)} %bitcast.130, bf16[512,4096]{1,0:T(8,128)(2,1)} %param.19), kind=kOutput, calls=%fused_computation.97 | convolution fusion | flops 2147483648 | bytes 13107200 | tf_op jit(solution)/shard_map/dot_general | solution.py:162
  557.2 79.5 %reduce-scatter.2.cloned.1.call-done = f32[512,1024]{1,0:T(8,128)} async-done(((f32[512,4096]{1,0:T(8,128)}), f32[512,1024]{1,0:T(8,128)}) %reduce-scatter.2.cloned.1.call-update) | async-done | bytes 2097168 | tf_op jit(solution)/shard_map/reduce_scatter | solution.py:163
  638.7 5.3 gather_fusion
  644.0 7.7 %all-to-all-start.2 = ((bf16[32,32,1024]{2,1,0:T(8,128)(2,1)}), bf16[32,32,1024]{2,1,0:T(8,128)(2,1)S(1)}, u32[]{:S(2)}, u32[]{:S(2)}) async-start(bf16[32,32,1024]{2,1,0:T(8,128)(2,1)} %bitcast.126), calls=%async_computation.3 | async-start | bytes 4194304 | tf_op jit(solution)/shard_map/all_to_all | solution.py:166
  651.7 28.3 %all-to-all-done.2 = bf16[32,32,1024]{2,1,0:T(8,128)(2,1)S(1)} async-done(((bf16[32,32,1024]{2,1,0:T(8,128)(2,1)}), bf16[32,32,1024]{2,1,0:T(8,128)(2,1)S(1)}, u32[]{:S(2)}, u32[]{:S(2)}) %all-to-all-start.2) | async-done | bytes 2097184 | tf_op jit(solution)/shard_map/all_to_all | solution.py:166
  (356 shorter events, 240.0 us)
Async XLA Ops:
  6.5 110.9 %copy-start = (bf16[4096,128]{1,0:T(8,128)(2,1)S(1)}, bf16[4096,128]{1,0:T(8,128)(2,1)}, u32[]{:S(2)}) copy-start(bf16[4096,128]{1,0:T(8,128)(2,1)} %param.17) | copy-start | bytes 3145732
  12.0 16.5 %all-to-all-start = ((s32[32,1,32]{2,1,0:T(1,128)}), s32[32,1,32]{2,1,0:T(1,128)S(1)}, u32[]{:S(2)}, u32[]{:S(2)}) async-start(s32[32,1,32]{2,1,0:T(1,128)} %all_to_all.12), calls=%async_computation | async-start | bytes 32768 | tf_op jit(solution)/shard_map/all_to_all | solution.py:65
  28.5 33.6 %all-to-all-start.1 = ((bf16[32,32,1024]{2,1,0:T(8,128)(2,1)}), bf16[32,32,1024]{2,1,0:T(8,128)(2,1)S(1)}, u32[]{:S(2)}, u32[]{:S(2)}) async-start(bf16[32,32,1024]{2,1,0:T(8,128)(2,1)} %bitcast.5), calls=%async_computation.1 | async-start | bytes 4194304 | tf_op jit(solution)/shard_map/all_to_all | solution.py:58
  33.9 83.6 %copy-start.7 = (f32[4096]{0:T(1024)S(1)}, f32[4096]{0:T(1024)}, u32[]{:S(2)}) copy-start(f32[4096]{0:T(1024)} %param.15) | copy-start | bytes 49156
  33.9 80.3 %all-gather.6.cloned.1.call-start = ((), (), s32[]{:S(2)}) async-start(), calls=%async_computation.4 | async-start | bytes 5242880 | tf_op jit(solution)/shard_map/all_gather | solution.py:75
  68.4 102.5 %all-gather.8.cloned.1.call-start = ((), (), s32[]{:S(2)}) async-start(), calls=%async_computation.5 | async-start | bytes 4325376 | tf_op jit(solution)/shard_map/all_gather | solution.py:129
  114.2 3.4 copy-start.3
  117.6 3.1 copy-start.6
  120.5 5.1 copy-start.5
  120.5 98.5 %all-gather.10.cloned.1.call-start = ((), (), s32[]{:S(2)}) async-start(), calls=%async_computation.7 | async-start | bytes 4325376 | tf_op jit(solution)/shard_map/all_gather | solution.py:130
  124.9 511.8 %reduce-scatter.2.cloned.1.call-start = ((), (), s32[]{:S(2)}) async-start(), calls=%async_computation.6 | async-start | bytes 10485760 | tf_op jit(solution)/shard_map/reduce_scatter | solution.py:163
  229.4 3.8 copy-start.1
  238.7 3.8 copy-start.1
  248.8 3.8 copy-start.1
  258.8 3.8 copy-start.1
  268.8 3.8 copy-start.1
  278.9 3.8 copy-start.1
  288.9 3.8 copy-start.1
  298.9 3.8 copy-start.1
  308.9 3.8 copy-start.1
  319.0 3.8 copy-start.1
  329.0 3.8 copy-start.1
  339.0 3.8 copy-start.1
  349.1 3.8 copy-start.1
  359.1 3.8 copy-start.1
  369.1 3.8 copy-start.1
  379.1 3.8 copy-start.1
  389.2 3.8 copy-start.1
  399.2 3.8 copy-start.1
  409.2 3.8 copy-start.1
  419.3 3.8 copy-start.1
  429.3 3.8 copy-start.1
  439.3 3.8 copy-start.1
  449.4 3.8 copy-start.1
  459.4 3.8 copy-start.1
  469.4 3.8 copy-start.1
  479.4 3.8 copy-start.1
  489.5 3.8 copy-start.1
  499.5 3.8 copy-start.1
  509.5 3.8 copy-start.1
  519.6 3.8 copy-start.1
  529.6 3.8 copy-start.1
  539.6 3.8 copy-start.1
  545.7 1.0 copy-start.4
  557.2 79.6 %copy-start.2 = (bf16[512,1024]{1,0:T(8,128)(2,1)S(1)}, bf16[512,1024]{1,0:T(8,128)(2,1)}, u32[]{:S(2)}) copy-start(bf16[512,1024]{1,0:T(8,128)(2,1)} %scatter_custom_fusion.2) | copy-start | bytes 3145732
  644.0 36.0 %all-to-all-start.2 = ((bf16[32,32,1024]{2,1,0:T(8,128)(2,1)}), bf16[32,32,1024]{2,1,0:T(8,128)(2,1)S(1)}, u32[]{:S(2)}, u32[]{:S(2)}) async-start(bf16[32,32,1024]{2,1,0:T(8,128)(2,1)} %bitcast.126), calls=%async_computation.3 | async-start | bytes 4194304 | tf_op jit(solution)/shard_map/all_to_all | solution.py:166
Sparse Core Ops, SparseCore 0:
  68.5 45.6 all-gather.5
  120.6 50.2 all-gather.7
  173.2 45.8 all-gather.9
  557.3 79.3 reduce-scatter.1
where the time goes:
time: 692 us; the launch traced here: 689 us
  matrix products  259 us (37%)
  waiting for transfers between devices  235 us (34%)
  other arithmetic  93.1 us (13%)
  local copies, waits for them, and re-layouts  37.1 us (5%)
  blocking collectives  24.9 us (4%)
  starting transfers between devices  22.9 us (3%)
  between operations  16.3 us (2%)
    dot_general x32, matrix products, attend_block(): jnp.einsum('grqk,kgd->grqd', exp_scores.astype(jnp.bfloat16), values_blk,...  122 us
    dot_general x32, matrix products, attend_block(): jnp.einsum('qgrd,kgd->grqk', queries, keys_blk, preferred_element_type=jn...  117 us
    reduce_scatter x1, waiting for transfers between devices, local(): lax.psum_scatter(partial_out, 'mp', scatter_dimension=1, tiled=True)  79.5 us
    all_gather x1, waiting for transfers between devices, local(): values_piece = lax.all_gather(values_own, 'dp', axis=0, tiled=True)  48.1 us
    all_gather x1, waiting for transfers between devices, local(): routed = lax.all_gather(routed_part, 'mp', axis=1, tiled=True)  45.7 us
    add x32, other arithmetic, attend_block(): row_total = row_total * rescale + jnp.sum(exp_scores, axis=-1)  41.2 us
    reduce_sum x32, other arithmetic, attend_block(): row_total = row_total * rescale + jnp.sum(exp_scores, axis=-1)  29.3 us
    all_to_all x1, waiting for transfers between devices, local(): lax.all_to_all(backward, 'dp', split_axis=0, concat_axis=0, tiled=True)  28.3 us
  transfers between devices with their start and end apart: 7, of which 7 were waited for; matrix products, arithmetic and copies ran while one was open for 4% of the time, Pallas kernels for 0%

commit v1 on v0

--- a/solution.py
+++ b/solution.py
@@ -127,7 +127,9 @@
     )
     first_row = jnp.int32(0)
     keys_piece = lax.all_gather(keys_own, "dp", axis=0, tiled=True)
-    values_piece = lax.all_gather(values_own, "dp", axis=0, tiled=True)
+    values_piece = jnp.concatenate(
+        jax.lax.all_to_all(jnp.stack([values_own] * jax.lax.psum(1, "dp")), "dp", 0, 0), 0
+    )
     ids_piece = lax.all_gather(doc_ids, "dp", axis=0, tiled=True)
     key_count = keys_piece.shape[0]
     block_len = math.gcd(key_count, key_block)

time: 692 us -> 692 us (level)
  waiting for transfers between devices: 235 us -> 182 us
  blocking collectives: 24.9 us -> 73.2 us
  starting transfers between devices: 22.9 us -> 30.8 us
    all_gather x1, blocking collectives: 24.9 us -> 73.2 us  [local(): ids_piece = lax.all_gather(doc_ids, 'dp', axis=0, tiled=True)]
    all_gather x1 -> x0, waiting for transfers between devices: 48.1 us -> none  [local(): values_piece = lax.all_gather(values_own, 'dp', axis=0, tiled=True)]
    all_to_all x0 -> x1, starting transfers between devices: none -> 7.93 us  [local(): jax.lax.all_to_all(jnp.stack([values_own] * jax.lax.psum(1, 'dp')), 'dp',...]
  transfers between devices with their start and end apart: 7 -> 7, of which waited for: 7 -> 5; matrix products, arithmetic and copies ran while one was open for 4% -> 3% of each run, Pallas kernels for 0% -> 0%
where the time goes in v1:
time: 692 us; the launch traced here: 689 us
  matrix products  258 us (37%)
  waiting for transfers between devices  182 us (26%)
  other arithmetic  91.3 us (13%)
  blocking collectives  73.2 us (11%)
  local copies, waits for them, and re-layouts  35.9 us (5%)
  starting transfers between devices  30.8 us (4%)
  between operations  16.4 us (2%)
    dot_general x32, matrix products, attend_block(): jnp.einsum('grqk,kgd->grqd', exp_scores.astype(jnp.bfloat16), values_blk,...  122 us
    dot_general x32, matrix products, attend_block(): jnp.einsum('qgrd,kgd->grqk', queries, keys_blk, preferred_element_type=jn...  117 us
    reduce_scatter x1, waiting for transfers between devices, local(): lax.psum_scatter(partial_out, 'mp', scatter_dimension=1, tiled=True)  78.9 us
    all_gather x1, blocking collectives, local(): ids_piece = lax.all_gather(doc_ids, 'dp', axis=0, tiled=True)  73.2 us
    all_gather x1, waiting for transfers between devices, local(): routed = lax.all_gather(routed_part, 'mp', axis=1, tiled=True)  45.5 us
    add x32, other arithmetic, attend_block(): row_total = row_total * rescale + jnp.sum(exp_scores, axis=-1)  41.2 us
    reduce_sum x32, other arithmetic, attend_block(): row_total = row_total * rescale + jnp.sum(exp_scores, axis=-1)  29.3 us
    all_to_all x1, waiting for transfers between devices, local(): lax.all_to_all(backward, 'dp', split_axis=0, concat_axis=0, tiled=True)  28.3 us
  transfers between devices with their start and end apart: 7, of which 5 were waited for; matrix products, arithmetic and copies ran while one was open for 3% of the time, Pallas kernels for 0%

profile of v1, /device:TPU:1, one launch (start us, length us, event | category | flops | bytes accessed | tf_op | source)
XLA Modules:
  0.0 688.9 jit_solution(15318927313271304495)
XLA Ops:
  12.0 9.6 %all-to-all-start = ((s32[32,1,32]{2,1,0:T(1,128)}), s32[32,1,32]{2,1,0:T(1,128)S(1)}, u32[]{:S(2)}, u32[]{:S(2)}) async-start(s32[32,1,32]{2,1,0:T(1,128)} %all_to_all.15), calls=%async_computation | async-start | bytes 32768 | tf_op jit(solution)/shard_map/all_to_all | solution.py:65
  21.6 4.8 scatter_custom_fusion.1
  28.5 5.3 all-to-all-start.1
  35.2 26.9 %all-to-all-done.1 = bf16[32,32,1024]{2,1,0:T(8,128)(2,1)S(1)} async-done(((bf16[32,32,1024]{2,1,0:T(8,128)(2,1)}), bf16[32,32,1024]{2,1,0:T(8,128)(2,1)S(1)}, u32[]{:S(2)}, u32[]{:S(2)}) %all-to-all-start.1) | async-done | bytes 2097184 | tf_op jit(solution)/shard_map/all_to_all | solution.py:58
  62.2 6.2 scatter_custom_fusion.2
  68.7 45.5 %all-gather.4.cloned.1.call-done = bf16[512,4096]{1,0:T(8,128)(2,1)} async-done(((bf16[512,1024]{1,0:T(8,128)(2,1)}), bf16[512,4096]{1,0:T(8,128)(2,1)}) %all-gather.4.cloned.1.call-update) | async-done | bytes 4194320 | tf_op jit(solution)/shard_map/all_gather | solution.py:75
  126.9 7.9 %all-to-all-start.2 = ((bf16[32,512,1,128]{3,1,2,0:T(8,128)(2,1)}), bf16[32,512,1,128]{3,1,2,0:T(8,128)(2,1)}, u32[]{:S(2)}, u32[]{:S(2)}) async-start(bf16[32,512,1,128]{3,1,2,0:T(8,128)(2,1)} %stack.3), calls=%async_computation.2 | async-start | bytes 8388608 | tf_op jit(solution)/shard_map/all_to_all | solution.py:131
  135.5 73.2 %all-gather = s32[32,1,512]{2,1,0:T(1,128)S(1)} all-gather(s32[1,1,512]{2,1,0:T(1,128)S(1)} %bitcast.135), channel_id=1, replica_groups=mesh['dp'=32,'mp'=4] {'dp'}, dimensions={0}, use_global_device_ids=true | all-gather | bytes 67584 | tf_op jit(solution)/shard_map/all_gather | solution.py:133
  213.9 5.9 fusion.49
  221.3 327.5 %conditional.1 = (f32[1,4,512]{2,1,0:T(4,128)}, f32[1,4,512,128]{2,3,1,0:T(8,128)S(1)}) conditional(s32[]{:T(128)} %bitcast.8, () %tuple.17, (bf16[16384,1,128]{0,2,1:T(8,128)(2,1)}, s32[16384]{0:T(1024)S(1)}, s32[512]{0:T(512)S(1)}, s32[512]{0:T(512)S(1)}, bf16[512,1,4,128]{3,0,2,1:T(8,128)(2,1)S(1)}, ...), branch_computations={%region_7.8_spmd, %region_8.13_spmd} | conditional | flops 550023168 | bytes 44123432 | solution.py:157
  221.5 6.4 copy.23
  227.9 320.5 %while.14 = (s32[]{:T(128)}, f32[1,4,512]{2,1,0:T(4,128)S(1)}, f32[1,4,512]{2,1,0:T(4,128)}, f32[1,4,512,128]{3,2,1,0:T(8,128)S(1)}, s32[512]{0:T(512)S(1)}, /*i...) while((s32[]{:T(128)}, f32[1,4,512]{2,1,0:T(4,128)S(1)}, ...), condition=%wide.region_12.12_spmd.clone, body=%wide.region_9.11_spmd.clone.sunk | while | flops 549990400 | bytes 33440936 | solution.py:152
  231.9 3.8 fusion.72
  241.3 3.8 fusion.72
  251.3 3.8 fusion.72
  261.4 3.8 fusion.72
  271.4 3.8 fusion.72
  281.4 3.8 fusion.72
  291.5 3.8 fusion.72
  301.5 3.8 fusion.72
  311.5 3.8 fusion.72
  321.6 3.8 fusion.72
  331.6 3.8 fusion.72
  341.7 3.8 fusion.72
  351.7 3.8 fusion.72
  361.7 3.8 fusion.72
  371.8 3.8 fusion.72
  381.8 3.8 fusion.72
  391.9 3.8 fusion.72
  401.9 3.8 fusion.72
  411.9 3.8 fusion.72
  422.0 3.8 fusion.72
  432.0 3.8 fusion.72
  442.0 3.8 fusion.72
  452.1 3.8 fusion.72
  462.1 3.8 fusion.72
  472.2 3.8 fusion.72
  482.2 3.8 fusion.72
  492.2 3.8 fusion.72
  502.3 3.8 fusion.72
  512.3 3.8 fusion.72
  522.3 3.8 fusion.72
  542.4 3.8 fusion.72
  549.6 7.8 %fusion.55 = f32[512,4096]{1,0:T(8,128)} fusion(bf16[512,512]{0,1:T(8,128)(2,1)S(1)} %bitcast.128, bf16[512,4096]{1,0:T(8,128)(2,1)} %param.19), kind=kOutput, calls=%fused_computation.97 | convolution fusion | flops 2147483648 | bytes 13107200 | tf_op jit(solution)/shard_map/dot_general | solution.py:164
  557.5 78.9 %reduce-scatter.2.cloned.1.call-done = f32[512,1024]{1,0:T(8,128)} async-done(((f32[512,4096]{1,0:T(8,128)}), f32[512,1024]{1,0:T(8,128)}) %reduce-scatter.2.cloned.1.call-update) | async-done | bytes 2097168 | tf_op jit(solution)/shard_map/reduce_scatter | solution.py:165
  638.3 5.3 gather_fusion
  643.7 7.6 %all-to-all-start.3 = ((bf16[32,32,1024]{2,1,0:T(8,128)(2,1)}), bf16[32,32,1024]{2,1,0:T(8,128)(2,1)S(1)}, u32[]{:S(2)}, u32[]{:S(2)}) async-start(bf16[32,32,1024]{2,1,0:T(8,128)(2,1)} %bitcast.124), calls=%async_computation.4 | async-start | bytes 4194304 | tf_op jit(solution)/shard_map/all_to_all | solution.py:168
  651.3 28.3 %all-to-all-done.3 = bf16[32,32,1024]{2,1,0:T(8,128)(2,1)S(1)} async-done(((bf16[32,32,1024]{2,1,0:T(8,128)(2,1)}), bf16[32,32,1024]{2,1,0:T(8,128)(2,1)S(1)}, u32[]{:S(2)}, u32[]{:S(2)}) %all-to-all-start.3) | async-done | bytes 2097184 | tf_op jit(solution)/shard_map/all_to_all | solution.py:168
  (356 shorter events, 233.1 us)
Async XLA Ops:
  6.5 110.9 %copy-start = (bf16[4096,128]{1,0:T(8,128)(2,1)S(1)}, bf16[4096,128]{1,0:T(8,128)(2,1)}, u32[]{:S(2)}) copy-start(bf16[4096,128]{1,0:T(8,128)(2,1)} %param.17) | copy-start | bytes 3145732
  12.0 16.5 %all-to-all-start = ((s32[32,1,32]{2,1,0:T(1,128)}), s32[32,1,32]{2,1,0:T(1,128)S(1)}, u32[]{:S(2)}, u32[]{:S(2)}) async-start(s32[32,1,32]{2,1,0:T(1,128)} %all_to_all.15), calls=%async_computation | async-start | bytes 32768 | tf_op jit(solution)/shard_map/all_to_all | solution.py:65
  28.5 33.7 %all-to-all-start.1 = ((bf16[32,32,1024]{2,1,0:T(8,128)(2,1)}), bf16[32,32,1024]{2,1,0:T(8,128)(2,1)S(1)}, u32[]{:S(2)}, u32[]{:S(2)}) async-start(bf16[32,32,1024]{2,1,0:T(8,128)(2,1)} %bitcast.4), calls=%async_computation.1 | async-start | bytes 4194304 | tf_op jit(solution)/shard_map/all_to_all | solution.py:58
  33.9 83.6 %copy-start.7 = (f32[4096]{0:T(1024)S(1)}, f32[4096]{0:T(1024)}, u32[]{:S(2)}) copy-start(f32[4096]{0:T(1024)} %param.15) | copy-start | bytes 49156
  33.9 80.3 %all-gather.4.cloned.1.call-start = ((), (), s32[]{:S(2)}) async-start(), calls=%async_computation.5 | async-start | bytes 5242880 | tf_op jit(solution)/shard_map/all_gather | solution.py:75
  68.4 152.9 %all-gather.6.cloned.1.call-start = ((), (), s32[]{:S(2)}) async-start(), calls=%async_computation.6 | async-start | bytes 4325376 | tf_op jit(solution)/shard_map/all_gather | solution.py:129
  114.2 3.4 copy-start.4
  117.6 2.9 copy-start.6
  126.9 8.6 %copy-start.5 = (s32[512]{0:T(512)S(1)}, s32[512]{0:T(512)}, u32[]{:S(2)}) copy-start(s32[512]{0:T(512)} %param.14) | copy-start | bytes 6148
  126.9 94.3 %all-to-all-start.2 = ((bf16[32,512,1,128]{3,1,2,0:T(8,128)(2,1)}), bf16[32,512,1,128]{3,1,2,0:T(8,128)(2,1)}, u32[]{:S(2)}, u32[]{:S(2)}) async-start(bf16[32,512,1,128]{3,1,2,0:T(8,128)(2,1)} %stack.3), calls=%async_computation.2 | async-start | bytes 8388608 | tf_op jit(solution)/shard_map/all_to_all | solution.py:131
  134.9 501.5 %reduce-scatter.2.cloned.1.call-start = ((), (), s32[]{:S(2)}) async-start(), calls=%async_computation.7 | async-start | bytes 10485760 | tf_op jit(solution)/shard_map/reduce_scatter | solution.py:165
  231.9 3.8 copy-start.2
  241.3 3.8 copy-start.2
  251.3 3.8 copy-start.2
  261.3 3.8 copy-start.2
  271.4 3.8 copy-start.2
  281.4 3.8 copy-start.2
  291.5 3.8 copy-start.2
  301.5 3.8 copy-start.2
  311.5 3.8 copy-start.2
  321.6 3.8 copy-start.2
  331.6 3.8 copy-start.2
  341.6 3.8 copy-start.2
  351.7 3.8 copy-start.2
  361.7 3.8 copy-start.2
  371.8 3.8 copy-start.2
  381.8 3.8 copy-start.2
  391.8 3.8 copy-start.2
  401.9 3.8 copy-start.2
  411.9 3.8 copy-start.2
  421.9 3.8 copy-start.2
  432.0 3.8 copy-start.2
  442.0 3.8 copy-start.2
  452.1 3.8 copy-start.2
  462.1 3.8 copy-start.2
  472.1 3.8 copy-start.2
  482.2 3.8 copy-start.2
  492.2 3.8 copy-start.2
  502.2 3.8 copy-start.2
  512.3 3.8 copy-start.2
  522.3 3.8 copy-start.2
  532.4 3.8 copy-start.2
  542.4 3.8 copy-start.2
  557.4 78.9 %copy-start.3 = (bf16[512,1024]{1,0:T(8,128)(2,1)S(1)}, bf16[512,1024]{1,0:T(8,128)(2,1)}, u32[]{:S(2)}) copy-start(bf16[512,1024]{1,0:T(8,128)(2,1)} %scatter_custom_fusion.2) | copy-start | bytes 3145732
  643.7 35.9 %all-to-all-start.3 = ((bf16[32,32,1024]{2,1,0:T(8,128)(2,1)}), bf16[32,32,1024]{2,1,0:T(8,128)(2,1)S(1)}, u32[]{:S(2)}, u32[]{:S(2)}) async-start(bf16[32,32,1024]{2,1,0:T(8,128)(2,1)} %bitcast.124), calls=%async_computation.4 | async-start | bytes 4194304 | tf_op jit(solution)/shard_map/all_to_all | solution.py:168
  679.6 2.8 copy-start.1
Sparse Core Ops, SparseCore 0:
  68.5 45.6 all-gather.3
  120.6 80.5 all-gather.5
  557.6 78.7 reduce-scatter.1
